TPU v7x, 256 devices: a whole 4x4x8 slice. The times are simulated.
256 devices in a mesh: tm: 8 (over y_lo, x), stn: 32 (over y_hi, z, core).
Axes of the slice: x: 4, y: 4 (y_hi: 2, y_lo: 2; y = y_hi * 2 + y_lo), z: 8, core: 2. Of those that a mesh axis runs over, the one named last changes fastest.
Arguments:
- voltages: bfloat16 [1024, 524288], P('stn', 'tm'), may hold values from -6 to 6
- gains: float32 [2, 1024, 256], P(None, 'stn'), may hold values from -4 to 4
Outputs:
- visibility: float32 [256, 2, 1024, 1024], P(('tm', 'stn'))
All inputs are finite; a program needn't handle non-finite values.
Results may differ from a plain program's by a relative error of at most 0.0038.
Values may be sent and summed in bfloat16 or wider, within the bound.
No kernel may reach another device: no remote copies, remote signals or barrier semaphores. Data moves between devices by JAX's collectives and lax.ppermute only.
A program may use at most 128 MiB of HBM per device.

v0:
```python
import functools

import numpy as np

import jax
import jax.numpy as jnp
from jax import lax
from jax.experimental import pallas as pl
from jax.experimental.pallas import tpu as pltpu
from jax.sharding import PartitionSpec as P

CHANNELS = 4096
BAND_LOW = 1024
TAPS = 8


def passed_along(x, axis, by):
    devices = lax.axis_size(axis)
    pairs = [(i, i + by) for i in range(devices) if 0 <= i + by < devices]
    return lax.ppermute(x, axis, pairs)


def window_table(chans):
    frame_len = 2 * chans
    total_len = TAPS * frame_len
    positions = np.arange(total_len, dtype=np.float64)
    centred = (positions - (total_len - 1) / 2.0) / frame_len
    taper = np.sin(np.pi * (positions + 0.5) / total_len)
    shaped = np.sinc(centred) * taper * taper
    shaped = shaped / np.sqrt(np.sum(shaped * shaped))
    return shaped.reshape(TAPS, frame_len).astype(np.float32)


def split(x):
    hi = lax.reduce_precision(x, exponent_bits=8, mantissa_bits=7)
    lo = x - hi
    return hi.astype(jnp.bfloat16), lo.astype(jnp.bfloat16)


def band_tables(frame_len, band):
    half = band // 2
    n_b = 32
    n_a = frame_len // 2 // n_b
    q = jnp.arange(2, dtype=jnp.int32)[:, None, None]
    k = jnp.arange(band, dtype=jnp.int32)[None, None, :]
    chan = 2 * (k % half) + q
    imag_col = k >= half
    a = jnp.arange(n_a, dtype=jnp.int32)[None, :, None]
    b = jnp.arange(n_b, dtype=jnp.int32)[None, :, None]
    p_steps = n_a * 2
    tp = (2.0 * jnp.pi / p_steps) * ((a * chan) % p_steps).astype(jnp.float32)
    tq = (2.0 * jnp.pi / frame_len) * ((b * (BAND_LOW + chan)) % frame_len).astype(jnp.float32)
    pr, pi = jnp.cos(tp), -jnp.sin(tp)
    qr, qi = jnp.cos(tq), -jnp.sin(tq)
    b1 = jnp.where(imag_col, qi, qr)
    b2 = jnp.where(imag_col, qr, -qi)
    t = pr[:, :, None, :] * b1[:, None, :, :] + pi[:, :, None, :] * b2[:, None, :, :]
    return t.reshape(2, n_a * n_b, band)


def taps_dft_kernel(x_ref, w_ref, table_hbm, out_ref, lhs_ref, table_ref, sem, *, first_slot, n_slots):
    step = pl.program_id(0)
    steps = pl.num_programs(0)
    block = x_ref.shape[0]
    inputs = block * steps
    frame_len = w_ref.shape[1]
    half = frame_len // 2
    frames = x_ref.shape[1] // frame_len
    history = TAPS - 1
    lanes = 128
    copy_table = pltpu.make_async_copy(table_hbm, table_ref, sem.at[0])

    @pl.when(step == 0)
    def _():
        copy_table.start()

    row0 = pl.multiple_of(step * block, block)

    def chunk(j, carry):
        base = pl.multiple_of(j * lanes, lanes)
        for r0 in range(0, block, 8):
            inputs_at = pl.ds(r0, 8)
            xs = []
            ws = []
            for offset in (0, half):
                xs.append([x_ref[inputs_at, pl.ds(f * frame_len + offset + base, lanes)].astype(jnp.float32) for f in range(frames)])
                ws.append([w_ref[pl.ds(p, 1), pl.ds(offset + base, lanes)] for p in range(TAPS)])
            for slot in range(n_slots):
                s = first_slot + slot
                accs = []
                for part in range(2):
                    acc = None
                    for p in range(TAPS):
                        g = s + p - history
                        if 0 <= g < frames:
                            term = ws[part][p] * xs[part][g]
                            acc = term if acc is None else acc + term
                    accs.append(acc)
                folded = (accs[0] + accs[1], accs[0] - accs[1])
                rows = pl.ds(pl.multiple_of(slot * inputs + row0 + r0, 8), 8)
                for q in range(2):
                    lhs_ref[q, rows, pl.ds(base, lanes)] = folded[q]
        return carry

    lax.fori_loop(0, half // lanes, chunk, 0)

    @pl.when(step == steps - 1)
    def _():
        copy_table.wait()
        depth = 512
        f32 = jnp.float32
        for q in range(2):
            out_ref[q] = jnp.zeros(out_ref.shape[1:], f32)

            def kstep(kk, carry):
                k0 = pl.multiple_of(kk * depth, depth)
                cols = pl.ds(k0, depth)
                folded = lhs_ref[q, :, cols]
                l_hi = folded.astype(jnp.bfloat16)
                l_lo = (folded - l_hi.astype(f32)).astype(jnp.bfloat16)
                table = table_ref[q, cols, :]
                t_hi = table.astype(jnp.bfloat16)
                t_lo = (table - t_hi.astype(f32)).astype(jnp.bfloat16)
                acc = jnp.dot(l_hi, t_hi, preferred_element_type=f32)
                acc = acc + jnp.dot(l_lo, t_hi, preferred_element_type=f32)
                acc = acc + jnp.dot(l_hi, t_lo, preferred_element_type=f32)
                out_ref[q] += acc
                return carry

            lax.fori_loop(0, half // depth, kstep, 0)


def band_spectra(voltages, window, table, frames, first_slot, n_slots):
    in_dev, length = voltages.shape
    frame_len = window.shape[1]
    half = frame_len // 2
    band = table.shape[2]
    block = 16
    rows = n_slots * in_dev
    kernel = functools.partial(taps_dft_kernel, first_slot=first_slot, n_slots=n_slots)
    return pl.pallas_call(
        kernel,
        out_shape=jax.ShapeDtypeStruct((2, rows, band), jnp.float32),
        grid=(in_dev // block,),
        in_specs=[
            pl.BlockSpec((block, length), lambda g: (g, 0)),
            pl.BlockSpec((TAPS, frame_len), lambda g: (0, 0)),
            pl.BlockSpec(memory_space=pl.ANY),
        ],
        out_specs=pl.BlockSpec((2, rows, band), lambda g: (0, 0, 0)),
        scratch_shapes=[
            pltpu.VMEM((2, rows, half), jnp.float32),
            pltpu.VMEM((2, half, band), jnp.float32),
            pltpu.SemaphoreType.DMA((1,)),
        ],
        compiler_params=pltpu.CompilerParams(vmem_limit_bytes=48 * 1024 * 1024),
    )(voltages, window, table)


def on_device(voltages, gains):
    in_dev, length = voltages.shape
    band = gains.shape[2]
    half_band = band // 2
    frame_len = 2 * CHANNELS
    frames = length // frame_len
    n_time = lax.axis_size("tm")
    n_station = lax.axis_size("stn")
    all_inputs = in_dev * n_station
    history = TAPS - 1
    window = jnp.asarray(window_table(CHANNELS))
    table = band_tables(frame_len, band)

    raw_next = band_spectra(voltages, window, table, frames, frames, history)
    given = passed_along(raw_next, "tm", 1)
    raw = band_spectra(voltages, window, table, frames, 0, frames)
    raw = raw.at[:, : history * in_dev, :].add(given)
    raw = jnp.transpose(raw, (0, 2, 1))

    row = frames * in_dev
    raw = jnp.transpose(raw.reshape(2, 2, half_band, row), (1, 2, 0, 3))
    raw_re, raw_im = raw[0], raw[1]
    g = jnp.transpose(gains.reshape(2, in_dev, half_band, 2), (0, 2, 3, 1))
    g = jnp.tile(g, (1, 1, 1, frames))
    gain_re, gain_im = g[0], g[1]
    spec_re = gain_re * raw_re - gain_im * raw_im
    spec_im = gain_re * raw_im + gain_im * raw_re
    spectra = jnp.stack([spec_re, spec_im], axis=2).astype(jnp.bfloat16)
    spectra = spectra.reshape(n_time * n_station, 2 * row)
    spectra = lax.all_to_all(spectra, ("tm", "stn"), split_axis=0, concat_axis=0, tiled=True)
    spectra = spectra.reshape(n_time, n_station, 2, frames, in_dev)
    stacked = jnp.transpose(spectra, (2, 0, 3, 1, 4)).reshape(2, n_time * frames, all_inputs)
    flipped = jnp.concatenate([stacked[1], -stacked[0]], axis=0)
    stacked = stacked.reshape(2 * n_time * frames, all_inputs)
    both = jnp.concatenate([stacked, flipped], axis=1)
    vis = jnp.einsum("ki,kj->ij", both, stacked, preferred_element_type=jnp.float32)
    vis = vis * (1.0 / float(n_time * frames))
    return vis.reshape(1, 2, all_inputs, all_inputs)


def solution(mesh):
    in_specs = (P("stn", "tm"), P(None, "stn", None))
    out_specs = P(("tm", "stn"), None, None, None)
    return jax.shard_map(
        on_device, mesh=mesh, in_specs=in_specs, out_specs=out_specs, check_vma=False
    )
```

profile of v0, /device:TPU:1, one launch (start us, length us, event | category | flops | bytes accessed | tf_op | source)
XLA Modules:
  0.0 73.8 jit_solution(15149785104235711629)
XLA Ops:
  0.0 0.0 copy-start.1
  0.0 0.0 copy-start
  0.0 1.0 %fusion.16 = (f32[2,128,256]{2,1,0:T(8,128)S(1)}, f32[2,128,256]{2,1,0:T(8,128)S(1)}) fusion(s32[2,256]{1,0:T(2,128)S(1)} %get-tuple-element.27), kind=kLoop, calls=%fused_computation.34 | loop fusion | flops 983040 | bytes 526336 | tf_op jit(solution)/shard_map/cos | solution.py:53
  1.1 0.3 negate_select_fusion.4
  1.4 4.6 %multiply_add_fusion = f32[2,128,32,256]{3,2,1,0:T(8,128)} fusion(f32[2,32,256]{2,1,0:T(8,128)S(1)} %get-tuple-element.24, f32[2,128,256]{2,1,0:T(8,128)S(1)} %get-tuple-element.26, f32[2,32,256]{2,1,0:T(8,128)S(1)} %get-tuple-element.23, f32[2,128,256]{2,1,0:T(8,128)S(1)} %get-tuple-element.25), kind=kLoop, calls=%fused_computation | loop fusion | flops 6291456 | bytes 9043968 | tf_op jit(solution)/shard_map/add | solution.py:57
  6.0 0.0 copy-done.1
  6.0 0.0 copy-done
  6.0 9.1 %shard_map.38 = f32[2,224,256]{2,1,0:T(8,128)S(1)} custom-call(bf16[32,65536]{1,0:T(8,128)(2,1)S(1)} %copy-done, f32[8,8192]{1,0:T(8,128)S(1)} %copy-done.1, f32[2,4096,256]{2,1,0:T(8,128)} %bitcast.55), custom_call_target="tpu_custom_call" | custom-call | tf_op jit(solution)/shard_map/pallas_call | solution.py:141
  15.1 0.0 copy-start.2
  15.1 4.1 %collective-permute-start = (f32[2,224,256]{2,1,0:T(8,128)S(1)}, f32[2,224,256]{2,1,0:T(8,128)S(1)}, u32[]{:S(2)}, u32[]{:S(2)}) collective-permute-start(f32[2,224,256]{2,1,0:T(8,128)S(1)} %shard_map.38), channel_id=1, source_target_pairs={{0,32},{32,64},{64,96},{96,128},{128,160},{160,192},{192,224},{1,3... | collective-permute-start | bytes 1376264 | tf_op jit(solution)/shard_map/ppermute | solution.py:20
  19.2 10.1 %shard_map.37 = f32[2,256,256]{2,1,0:T(8,128)S(1)} custom-call(bf16[32,65536]{1,0:T(8,128)(2,1)S(1)} %copy-done, f32[8,8192]{1,0:T(8,128)S(1)} %copy-done.1, f32[2,4096,256]{2,1,0:T(8,128)} %bitcast.56), custom_call_target="tpu_custom_call" | custom-call | tf_op jit(solution)/shard_map/pallas_call | solution.py:141
  29.2 0.0 copy-done.2
  29.3 0.1 copy.20
  29.4 0.1 copy.21
  29.5 0.1 copy.23
  29.6 0.0 collective-permute-done
  29.6 0.1 fusion.5
  29.7 0.1 fusion.10
  29.9 0.2 copy.24
  30.1 0.2 convert_element_type.39
  30.3 0.5 broadcast.255
  30.8 2.2 %reduce.3 = bf16[256,512]{1,0:T(8,128)(2,1)S(1)} reduce(bf16[256,1,512]{2,1,0:T(2,128)(2,1)S(1)} %convert_element_type.39, bf16[]{:T(256)} %broadcast.255), dimensions={1}, to_apply=%convert_element_type.39.reduce_sub_computation | reduce | bytes 524290 | tf_op jit(solution)/shard_map/convert_element_type | solution.py:187
  33.0 0.1 reshape.293
  33.1 30.9 %all_to_all.6 = bf16[256,2,256]{2,1,0:T(2,128)(2,1)S(1)} all-to-all(bf16[256,2,256]{2,1,0:T(2,128)(2,1)S(1)} %reshape.293), channel_id=1, replica_groups=mesh['tm'=8,'stn'=32] {'tm','stn'}, dimensions={0} | all-to-all | bytes 524288 | tf_op jit(solution)/shard_map/all_to_all | solution.py:189
  64.0 0.2 reshape.294
  64.2 1.6 %reduce.2 = bf16[256,512]{1,0:T(8,128)(2,1)S(1)} reduce(bf16[256,1,512]{2,1,0:T(2,128)(2,1)S(1)} %reshape.294, bf16[]{:T(256)} %constant.84), dimensions={1}, to_apply=%all_to_all.4.reduce_sub_computation | reduce | bytes 524290 | tf_op jit(solution)/shard_map/all_to_all | solution.py:189
  65.8 0.6 reshape.290
  66.3 0.1 fusion.28
  66.5 0.3 copy.26
  66.8 0.1 copy.28
  66.9 0.5 neg.28
  67.4 0.1 copy.27
  67.5 0.5 squeeze.14
  68.1 1.1 %reshape_reshape.3 = bf16[128,1024]{1,0:T(8,128)(2,1)S(1)} reshape(bf16[2,8,8,32,32]{4,3,2,1,0:T(8,128)(2,1)S(1)} %copy.26) | data formatting | bytes 524288 | tf_op jit(solution)/shard_map/reshape;reshape | solution.py:193
  69.1 4.7 %convolution_multiply_fusion = f32[2048,1024]{1,0:T(8,128)} fusion(bf16[128,1024]{1,0:T(8,128)(2,1)S(1)} %reshape_reshape.3, bf16[64,1024]{1,0:T(8,128)(2,1)S(1)} %neg.28, bf16[64,1024]{1,0:T(8,128)(2,1)S(1)} %squeeze.14), kind=kOutput, calls=%fused_computation.1 | convolution fusion | flops 540540928 | bytes 8912896 | tf_op jit(solution)/shard_map/ki,kj->ij/dot_general | solution.py:195
  (6 shorter events, 0.1 us)
Async XLA Ops:
  0.0 6.0 %copy-start.1 = (f32[8,8192]{1,0:T(8,128)S(1)}, f32[8,8192]{1,0:T(8,128)}, u32[]{:S(2)}) copy-start(f32[8,8192]{1,0:T(8,128)} %constant.83.clone.w_ref) | copy-start | bytes 786436
  0.0 6.0 %copy-start = (bf16[32,65536]{1,0:T(8,128)(2,1)S(1)}, bf16[32,65536]{1,0:T(8,128)(2,1)}, u32[]{:S(2)}) copy-start(bf16[32,65536]{1,0:T(8,128)(2,1)} %x_ref.3) | copy-start | bytes 12582916
  15.1 14.2 %copy-start.2 = (f32[2,32,256]{2,1,0:T(8,128)S(1)}, f32[2,32,256]{2,1,0:T(8,128)}, u32[]{:S(2)}) copy-start(f32[2,32,256]{2,1,0:T(8,128)} %param.6) | copy-start | bytes 196612
  15.1 14.5 %collective-permute-start = (f32[2,224,256]{2,1,0:T(8,128)S(1)}, f32[2,224,256]{2,1,0:T(8,128)S(1)}, u32[]{:S(2)}, u32[]{:S(2)}) collective-permute-start(f32[2,224,256]{2,1,0:T(8,128)S(1)} %shard_map.38), channel_id=1, source_target_pairs={{0,32},{32,64},{64,96},{96,128},{128,160},{160,192},{192,224},{1,3... | collective-permute-start | bytes 1376264 | tf_op jit(solution)/shard_map/ppermute | solution.py:20
where the time goes:
time: 74 us; the launch traced here: 73.8 us
  blocking collectives  30.9 us (42%)
  Pallas kernels  19.2 us (26%)
  other arithmetic  10.1 us (14%)
  local copies, waits for them, and re-layouts  4.76 us (6%)
  matrix products  4.68 us (6%)
  starting transfers between devices  4.06 us (5%)
    all_to_all x1, blocking collectives, on_device(): lax.all_to_all(spectra, ('tm', 'stn'), split_axis=0, concat_axis=0, tiled...  30.9 us
    pallas_call x2, Pallas kernels, band_spectra(): pl.pallas_call(kernel, out_shape=jax.ShapeDtypeStruct((2, rows, band), jn...  19.2 us
    dot_general x1, matrix products, on_device(): jnp.einsum('ki,kj->ij', both, stacked, preferred_element_type=jnp.float32)  4.68 us
    add x1, other arithmetic, band_tables(): pr[:, :, None, :] * b1[:, None, :, :]  4.58 us
    ppermute x1, starting transfers between devices, passed_along(): return lax.ppermute(x, axis, pairs)  4.06 us
    convert_element_type x1, other arithmetic, on_device(): spectra = jnp.stack([spec_re, spec_im], axis=2).astype(jnp.bfloat16)  2.21 us
    all_to_all x1, other arithmetic, on_device(): lax.all_to_all(spectra, ('tm', 'stn'), split_axis=0, concat_axis=0, tiled...  1.56 us
  transfers between devices with their start and end apart: 1, of which 0 were waited for; matrix products, arithmetic and copies ran while one was open for 0% of the time, Pallas kernels for 14%

commit v1 on v0

--- a/solution.py
+++ b/solution.py
@@ -96,10 +96,9 @@
                             term = ws[part][p] * xs[part][g]
                             acc = term if acc is None else acc + term
                     accs.append(acc)
-                folded = (accs[0] + accs[1], accs[0] - accs[1])
                 rows = pl.ds(pl.multiple_of(slot * inputs + row0 + r0, 8), 8)
-                for q in range(2):
-                    lhs_ref[q, rows, pl.ds(base, lanes)] = folded[q]
+                lhs_ref[rows, pl.ds(base, lanes)] = accs[0]
+                lhs_ref[rows, pl.ds(half + base, lanes)] = accs[1]
         return carry
 
     lax.fori_loop(0, half // lanes, chunk, 0)
@@ -109,13 +108,14 @@
         copy_table.wait()
         depth = 512
         f32 = jnp.float32
-        for q in range(2):
-            out_ref[q] = jnp.zeros(out_ref.shape[1:], f32)
-
-            def kstep(kk, carry):
-                k0 = pl.multiple_of(kk * depth, depth)
-                cols = pl.ds(k0, depth)
-                folded = lhs_ref[q, :, cols]
+        out_ref[...] = jnp.zeros(out_ref.shape, f32)
+
+        def kstep(kk, carry):
+            k0 = pl.multiple_of(kk * depth, depth)
+            cols = pl.ds(k0, depth)
+            first = lhs_ref[:, cols]
+            second = lhs_ref[:, pl.ds(half + k0, depth)]
+            for q, folded in enumerate((first + second, first - second)):
                 l_hi = folded.astype(jnp.bfloat16)
                 l_lo = (folded - l_hi.astype(f32)).astype(jnp.bfloat16)
                 table = table_ref[q, cols, :]
@@ -125,9 +125,9 @@
                 acc = acc + jnp.dot(l_lo, t_hi, preferred_element_type=f32)
                 acc = acc + jnp.dot(l_hi, t_lo, preferred_element_type=f32)
                 out_ref[q] += acc
-                return carry
-
-            lax.fori_loop(0, half // depth, kstep, 0)
+            return carry
+
+        lax.fori_loop(0, half // depth, kstep, 0)
 
 
 def band_spectra(voltages, window, table, frames, first_slot, n_slots):
@@ -149,7 +149,7 @@
         ],
         out_specs=pl.BlockSpec((2, rows, band), lambda g: (0, 0, 0)),
         scratch_shapes=[
-            pltpu.VMEM((2, rows, half), jnp.float32),
+            pltpu.VMEM((rows, frame_len), jnp.float32),
             pltpu.VMEM((2, half, band), jnp.float32),
             pltpu.SemaphoreType.DMA((1,)),
         ],

time: 74 us -> 73 us (0.986)
  Pallas kernels: 19.2 us -> 17.1 us
  blocking collectives: 30.9 us -> 31.9 us
    pallas_call x2, Pallas kernels: 19.2 us -> 17.1 us  [band_spectra(): pl.pallas_call(kernel, out_shape=jax.ShapeDtypeStruct((2, rows, band), jn...]
    all_to_all x1, blocking collectives: 30.9 us -> 31.9 us  [on_device(): lax.all_to_all(spectra, ('tm', 'stn'), split_axis=0, concat_axis=0, tiled...]
  transfers between devices with their start and end apart: 1 -> 1, of which waited for: 0 -> 0; matrix products, arithmetic and copies ran while one was open for 0% -> 0% of each run, Pallas kernels for 14% -> 12%
where the time goes in v1:
time: 73 us; the launch traced here: 72.8 us
  blocking collectives  31.9 us (44%)
  Pallas kernels  17.1 us (23%)
  other arithmetic  10.1 us (14%)
  local copies, waits for them, and re-layouts  4.76 us (7%)
  matrix products  4.67 us (6%)
  starting transfers between devices  4.09 us (6%)
    all_to_all x1, blocking collectives, on_device(): lax.all_to_all(spectra, ('tm', 'stn'), split_axis=0, concat_axis=0, tiled...  31.9 us
    pallas_call x2, Pallas kernels, band_spectra(): pl.pallas_call(kernel, out_shape=jax.ShapeDtypeStruct((2, rows, band), jn...  17.1 us
    dot_general x1, matrix products, on_device(): jnp.einsum('ki,kj->ij', both, stacked, preferred_element_type=jnp.float32)  4.67 us
    add x1, other arithmetic, band_tables(): pr[:, :, None, :] * b1[:, None, :, :]  4.58 us
    ppermute x1, starting transfers between devices, passed_along(): return lax.ppermute(x, axis, pairs)  4.09 us
    convert_element_type x1, other arithmetic, on_device(): spectra = jnp.stack([spec_re, spec_im], axis=2).astype(jnp.bfloat16)  2.21 us
    all_to_all x1, other arithmetic, on_device(): lax.all_to_all(spectra, ('tm', 'stn'), split_axis=0, concat_axis=0, tiled...  1.56 us
  transfers between devices with their start and end apart: 1, of which 0 were waited for; matrix products, arithmetic and copies ran while one was open for 0% of the time, Pallas kernels for 12%

profile of v1, /device:TPU:1, one launch (start us, length us, event | category | flops | bytes accessed | tf_op | source)
XLA Modules:
  0.0 72.8 jit_solution(12991412256480853494)
XLA Ops:
  0.0 0.0 copy-start.1
  0.0 0.0 copy-start
  0.0 1.0 %fusion.16 = (f32[2,128,256]{2,1,0:T(8,128)S(1)}, f32[2,128,256]{2,1,0:T(8,128)S(1)}) fusion(s32[2,256]{1,0:T(2,128)S(1)} %get-tuple-element.27), kind=kLoop, calls=%fused_computation.34 | loop fusion | flops 983040 | bytes 526336 | tf_op jit(solution)/shard_map/cos | solution.py:53
  1.1 0.3 negate_select_fusion.4
  1.4 4.6 %multiply_add_fusion = f32[2,128,32,256]{3,2,1,0:T(8,128)} fusion(f32[2,32,256]{2,1,0:T(8,128)S(1)} %get-tuple-element.24, f32[2,128,256]{2,1,0:T(8,128)S(1)} %get-tuple-element.26, f32[2,32,256]{2,1,0:T(8,128)S(1)} %get-tuple-element.23, f32[2,128,256]{2,1,0:T(8,128)S(1)} %get-tuple-element.25), kind=kLoop, calls=%fused_computation | loop fusion | flops 6291456 | bytes 9043968 | tf_op jit(solution)/shard_map/add | solution.py:57
  6.0 0.0 copy-done.1
  6.0 0.0 copy-done
  6.0 8.1 %shard_map.38 = f32[2,224,256]{2,1,0:T(8,128)S(1)} custom-call(bf16[32,65536]{1,0:T(8,128)(2,1)S(1)} %copy-done, f32[8,8192]{1,0:T(8,128)S(1)} %copy-done.1, f32[2,4096,256]{2,1,0:T(8,128)} %bitcast.55), custom_call_target="tpu_custom_call" | custom-call | tf_op jit(solution)/shard_map/pallas_call | solution.py:141
  14.0 0.0 copy-start.2
  14.0 4.1 %collective-permute-start = (f32[2,224,256]{2,1,0:T(8,128)S(1)}, f32[2,224,256]{2,1,0:T(8,128)S(1)}, u32[]{:S(2)}, u32[]{:S(2)}) collective-permute-start(f32[2,224,256]{2,1,0:T(8,128)S(1)} %shard_map.38), channel_id=1, source_target_pairs={{0,32},{32,64},{64,96},{96,128},{128,160},{160,192},{192,224},{1,3... | collective-permute-start | bytes 1376264 | tf_op jit(solution)/shard_map/ppermute | solution.py:20
  18.1 9.0 %shard_map.37 = f32[2,256,256]{2,1,0:T(8,128)S(1)} custom-call(bf16[32,65536]{1,0:T(8,128)(2,1)S(1)} %copy-done, f32[8,8192]{1,0:T(8,128)S(1)} %copy-done.1, f32[2,4096,256]{2,1,0:T(8,128)} %bitcast.56), custom_call_target="tpu_custom_call" | custom-call | tf_op jit(solution)/shard_map/pallas_call | solution.py:141
  27.2 0.0 copy-done.2
  27.2 0.1 copy.20
  27.3 0.1 copy.21
  27.4 0.1 copy.23
  27.5 0.0 collective-permute-done
  27.5 0.1 fusion.5
  27.7 0.1 fusion.10
  27.8 0.2 copy.24
  28.0 0.2 convert_element_type.39
  28.2 0.5 broadcast.255
  28.7 2.2 %reduce.3 = bf16[256,512]{1,0:T(8,128)(2,1)S(1)} reduce(bf16[256,1,512]{2,1,0:T(2,128)(2,1)S(1)} %convert_element_type.39, bf16[]{:T(256)} %broadcast.255), dimensions={1}, to_apply=%convert_element_type.39.reduce_sub_computation | reduce | bytes 524290 | tf_op jit(solution)/shard_map/convert_element_type | solution.py:187
  30.9 0.1 reshape.293
  31.0 31.9 %all_to_all.6 = bf16[256,2,256]{2,1,0:T(2,128)(2,1)S(1)} all-to-all(bf16[256,2,256]{2,1,0:T(2,128)(2,1)S(1)} %reshape.293), channel_id=1, replica_groups=mesh['tm'=8,'stn'=32] {'tm','stn'}, dimensions={0} | all-to-all | bytes 524288 | tf_op jit(solution)/shard_map/all_to_all | solution.py:189
  62.9 0.2 reshape.294
  63.2 1.6 %reduce.2 = bf16[256,512]{1,0:T(8,128)(2,1)S(1)} reduce(bf16[256,1,512]{2,1,0:T(2,128)(2,1)S(1)} %reshape.294, bf16[]{:T(256)} %constant.84), dimensions={1}, to_apply=%all_to_all.4.reduce_sub_computation | reduce | bytes 524290 | tf_op jit(solution)/shard_map/all_to_all | solution.py:189
  64.7 0.6 reshape.290
  65.3 0.1 fusion.28
  65.5 0.3 copy.26
  65.8 0.1 copy.28
  65.8 0.5 neg.28
  66.4 0.1 copy.27
  66.5 0.5 squeeze.14
  67.0 1.1 %reshape_reshape.3 = bf16[128,1024]{1,0:T(8,128)(2,1)S(1)} reshape(bf16[2,8,8,32,32]{4,3,2,1,0:T(8,128)(2,1)S(1)} %copy.26) | data formatting | bytes 524288 | tf_op jit(solution)/shard_map/reshape;reshape | solution.py:193
  68.1 4.7 %convolution_multiply_fusion = f32[2048,1024]{1,0:T(8,128)} fusion(bf16[128,1024]{1,0:T(8,128)(2,1)S(1)} %reshape_reshape.3, bf16[64,1024]{1,0:T(8,128)(2,1)S(1)} %neg.28, bf16[64,1024]{1,0:T(8,128)(2,1)S(1)} %squeeze.14), kind=kOutput, calls=%fused_computation.1 | convolution fusion | flops 540540928 | bytes 8912896 | tf_op jit(solution)/shard_map/ki,kj->ij/dot_general | solution.py:195
  (6 shorter events, 0.1 us)
Async XLA Ops:
  0.0 6.0 %copy-start.1 = (f32[8,8192]{1,0:T(8,128)S(1)}, f32[8,8192]{1,0:T(8,128)}, u32[]{:S(2)}) copy-start(f32[8,8192]{1,0:T(8,128)} %constant.83.clone.w_ref) | copy-start | bytes 786436
  0.0 6.0 %copy-start = (bf16[32,65536]{1,0:T(8,128)(2,1)S(1)}, bf16[32,65536]{1,0:T(8,128)(2,1)}, u32[]{:S(2)}) copy-start(bf16[32,65536]{1,0:T(8,128)(2,1)} %x_ref.3) | copy-start | bytes 12582916
  14.0 13.1 %copy-start.2 = (f32[2,32,256]{2,1,0:T(8,128)S(1)}, f32[2,32,256]{2,1,0:T(8,128)}, u32[]{:S(2)}) copy-start(f32[2,32,256]{2,1,0:T(8,128)} %param.6) | copy-start | bytes 196612
  14.0 13.4 %collective-permute-start = (f32[2,224,256]{2,1,0:T(8,128)S(1)}, f32[2,224,256]{2,1,0:T(8,128)S(1)}, u32[]{:S(2)}, u32[]{:S(2)}) collective-permute-start(f32[2,224,256]{2,1,0:T(8,128)S(1)} %shard_map.38), channel_id=1, source_target_pairs={{0,32},{32,64},{64,96},{96,128},{128,160},{160,192},{192,224},{1,3... | collective-permute-start | bytes 1376264 | tf_op jit(solution)/shard_map/ppermute | solution.py:20

commit v2 on v1

--- a/solution.py
+++ b/solution.py
@@ -106,7 +106,7 @@
     @pl.when(step == steps - 1)
     def _():
         copy_table.wait()
-        depth = 512
+        depth = 1024
         f32 = jnp.float32
         out_ref[...] = jnp.zeros(out_ref.shape, f32)
 

time: 73 us -> 72.3 us (level)
  Pallas kernels: 17.1 us -> 15.8 us
    pallas_call x2, Pallas kernels: 17.1 us -> 15.8 us  [band_spectra(): pl.pallas_call(kernel, out_shape=jax.ShapeDtypeStruct((2, rows, band), jn...]
  transfers between devices with their start and end apart: 1 -> 1, of which waited for: 0 -> 1; matrix products, arithmetic and copies ran while one was open for 0% -> 0% of each run, Pallas kernels for 12% -> 12%
where the time goes in v2:
time: 72.3 us; the launch traced here: 72.2 us
  blocking collectives  32.1 us (44%)
  Pallas kernels  15.8 us (22%)
  other arithmetic  10 us (14%)
  local copies, waits for them, and re-layouts  4.76 us (7%)
  matrix products  4.68 us (6%)
  starting transfers between devices  4.09 us (6%)
    all_to_all x1, blocking collectives, on_device(): lax.all_to_all(spectra, ('tm', 'stn'), split_axis=0, concat_axis=0, tiled...  32.1 us
    pallas_call x2, Pallas kernels, band_spectra(): pl.pallas_call(kernel, out_shape=jax.ShapeDtypeStruct((2, rows, band), jn...  15.8 us
    dot_general x1, matrix products, on_device(): jnp.einsum('ki,kj->ij', both, stacked, preferred_element_type=jnp.float32)  4.68 us
    add x1, other arithmetic, band_tables(): pr[:, :, None, :] * b1[:, None, :, :]  4.58 us
    ppermute x1, starting transfers between devices, passed_along(): return lax.ppermute(x, axis, pairs)  4.09 us
    convert_element_type x1, other arithmetic, on_device(): spectra = jnp.stack([spec_re, spec_im], axis=2).astype(jnp.bfloat16)  2.21 us
    all_to_all x1, other arithmetic, on_device(): lax.all_to_all(spectra, ('tm', 'stn'), split_axis=0, concat_axis=0, tiled...  1.56 us
  transfers between devices with their start and end apart: 1, of which 1 were waited for; matrix products, arithmetic and copies ran while one was open for 0% of the time, Pallas kernels for 12%

profile of v2, /device:TPU:1, one launch (start us, length us, event | category | flops | bytes accessed | tf_op | source)
XLA Modules:
  0.0 72.2 jit_solution(10571207577935632648)
XLA Ops:
  0.0 0.0 copy-start.1
  0.0 0.0 copy-start
  0.0 1.0 %fusion.16 = (f32[2,128,256]{2,1,0:T(8,128)S(1)}, f32[2,128,256]{2,1,0:T(8,128)S(1)}) fusion(s32[2,256]{1,0:T(2,128)S(1)} %get-tuple-element.27), kind=kLoop, calls=%fused_computation.34 | loop fusion | flops 983040 | bytes 526336 | tf_op jit(solution)/shard_map/cos | solution.py:53
  1.1 0.3 negate_select_fusion.4
  1.4 4.6 %multiply_add_fusion = f32[2,128,32,256]{3,2,1,0:T(8,128)} fusion(f32[2,32,256]{2,1,0:T(8,128)S(1)} %get-tuple-element.24, f32[2,128,256]{2,1,0:T(8,128)S(1)} %get-tuple-element.26, f32[2,32,256]{2,1,0:T(8,128)S(1)} %get-tuple-element.23, f32[2,128,256]{2,1,0:T(8,128)S(1)} %get-tuple-element.25), kind=kLoop, calls=%fused_computation | loop fusion | flops 6291456 | bytes 9043968 | tf_op jit(solution)/shard_map/add | solution.py:57
  6.0 0.0 copy-done.1
  6.0 0.0 copy-done
  6.0 7.4 %shard_map.38 = f32[2,224,256]{2,1,0:T(8,128)S(1)} custom-call(bf16[32,65536]{1,0:T(8,128)(2,1)S(1)} %copy-done, f32[8,8192]{1,0:T(8,128)S(1)} %copy-done.1, f32[2,4096,256]{2,1,0:T(8,128)} %bitcast.55), custom_call_target="tpu_custom_call" | custom-call | tf_op jit(solution)/shard_map/pallas_call | solution.py:141
  13.4 0.0 copy-start.2
  13.4 4.1 %collective-permute-start = (f32[2,224,256]{2,1,0:T(8,128)S(1)}, f32[2,224,256]{2,1,0:T(8,128)S(1)}, u32[]{:S(2)}, u32[]{:S(2)}) collective-permute-start(f32[2,224,256]{2,1,0:T(8,128)S(1)} %shard_map.38), channel_id=1, source_target_pairs={{0,32},{32,64},{64,96},{96,128},{128,160},{160,192},{192,224},{1,3... | collective-permute-start | bytes 1376264 | tf_op jit(solution)/shard_map/ppermute | solution.py:20
  17.5 8.4 %shard_map.37 = f32[2,256,256]{2,1,0:T(8,128)S(1)} custom-call(bf16[32,65536]{1,0:T(8,128)(2,1)S(1)} %copy-done, f32[8,8192]{1,0:T(8,128)S(1)} %copy-done.1, f32[2,4096,256]{2,1,0:T(8,128)} %bitcast.56), custom_call_target="tpu_custom_call" | custom-call | tf_op jit(solution)/shard_map/pallas_call | solution.py:141
  25.9 0.0 copy-done.2
  25.9 0.1 copy.20
  26.1 0.1 copy.21
  26.1 0.1 copy.23
  26.2 0.5 collective-permute-done
  26.7 0.1 fusion.5
  26.8 0.1 fusion.10
  27.0 0.2 copy.24
  27.1 0.2 convert_element_type.39
  27.4 0.5 broadcast.255
  27.9 2.2 %reduce.3 = bf16[256,512]{1,0:T(8,128)(2,1)S(1)} reduce(bf16[256,1,512]{2,1,0:T(2,128)(2,1)S(1)} %convert_element_type.39, bf16[]{:T(256)} %broadcast.255), dimensions={1}, to_apply=%convert_element_type.39.reduce_sub_computation | reduce | bytes 524290 | tf_op jit(solution)/shard_map/convert_element_type | solution.py:187
  30.1 0.1 reshape.293
  30.2 32.1 %all_to_all.6 = bf16[256,2,256]{2,1,0:T(2,128)(2,1)S(1)} all-to-all(bf16[256,2,256]{2,1,0:T(2,128)(2,1)S(1)} %reshape.293), channel_id=1, replica_groups=mesh['tm'=8,'stn'=32] {'tm','stn'}, dimensions={0} | all-to-all | bytes 524288 | tf_op jit(solution)/shard_map/all_to_all | solution.py:189
  62.3 0.2 reshape.294
  62.5 1.6 %reduce.2 = bf16[256,512]{1,0:T(8,128)(2,1)S(1)} reduce(bf16[256,1,512]{2,1,0:T(2,128)(2,1)S(1)} %reshape.294, bf16[]{:T(256)} %constant.84), dimensions={1}, to_apply=%all_to_all.4.reduce_sub_computation | reduce | bytes 524290 | tf_op jit(solution)/shard_map/all_to_all | solution.py:189
  64.1 0.6 reshape.290
  64.7 0.1 fusion.28
  64.9 0.3 copy.26
  65.1 0.1 copy.28
  65.2 0.5 neg.28
  65.8 0.1 copy.27
  65.9 0.5 squeeze.14
  66.4 1.1 %reshape_reshape.3 = bf16[128,1024]{1,0:T(8,128)(2,1)S(1)} reshape(bf16[2,8,8,32,32]{4,3,2,1,0:T(8,128)(2,1)S(1)} %copy.26) | data formatting | bytes 524288 | tf_op jit(solution)/shard_map/reshape;reshape | solution.py:193
  67.5 4.7 %convolution_multiply_fusion = f32[2048,1024]{1,0:T(8,128)} fusion(bf16[128,1024]{1,0:T(8,128)(2,1)S(1)} %reshape_reshape.3, bf16[64,1024]{1,0:T(8,128)(2,1)S(1)} %neg.28, bf16[64,1024]{1,0:T(8,128)(2,1)S(1)} %squeeze.14), kind=kOutput, calls=%fused_computation.1 | convolution fusion | flops 540540928 | bytes 8912896 | tf_op jit(solution)/shard_map/ki,kj->ij/dot_general | solution.py:195
  (6 shorter events, 0.1 us)
Async XLA Ops:
  0.0 6.0 %copy-start.1 = (f32[8,8192]{1,0:T(8,128)S(1)}, f32[8,8192]{1,0:T(8,128)}, u32[]{:S(2)}) copy-start(f32[8,8192]{1,0:T(8,128)} %constant.83.clone.w_ref) | copy-start | bytes 786436
  0.0 6.0 %copy-start = (bf16[32,65536]{1,0:T(8,128)(2,1)S(1)}, bf16[32,65536]{1,0:T(8,128)(2,1)}, u32[]{:S(2)}) copy-start(bf16[32,65536]{1,0:T(8,128)(2,1)} %x_ref.3) | copy-start | bytes 12582916
  13.4 12.5 %copy-start.2 = (f32[2,32,256]{2,1,0:T(8,128)S(1)}, f32[2,32,256]{2,1,0:T(8,128)}, u32[]{:S(2)}) copy-start(f32[2,32,256]{2,1,0:T(8,128)} %param.6) | copy-start | bytes 196612
  13.4 13.3 %collective-permute-start = (f32[2,224,256]{2,1,0:T(8,128)S(1)}, f32[2,224,256]{2,1,0:T(8,128)S(1)}, u32[]{:S(2)}, u32[]{:S(2)}) collective-permute-start(f32[2,224,256]{2,1,0:T(8,128)S(1)} %shard_map.38), channel_id=1, source_target_pairs={{0,32},{32,64},{64,96},{96,128},{128,160},{160,192},{192,224},{1,3... | collective-permute-start | bytes 1376264 | tf_op jit(solution)/shard_map/ppermute | solution.py:20

commit v3 on v2

--- a/solution.py
+++ b/solution.py
@@ -106,7 +106,7 @@
     @pl.when(step == steps - 1)
     def _():
         copy_table.wait()
-        depth = 1024
+        depth = 2048
         f32 = jnp.float32
         out_ref[...] = jnp.zeros(out_ref.shape, f32)
 

time: 72.3 us -> 72 us (level)
  transfers between devices with their start and end apart: 1 -> 1, of which waited for: 1 -> 1; matrix products, arithmetic and copies ran while one was open for 0% -> 0% of each run, Pallas kernels for 12% -> 11%
where the time goes in v3:
time: 72 us; the launch traced here: 71.9 us
  blocking collectives  32.1 us (45%)
  Pallas kernels  15.2 us (21%)
  other arithmetic  10 us (14%)
  local copies, waits for them, and re-layouts  4.76 us (7%)
  matrix products  4.67 us (6%)
  starting transfers between devices  4.09 us (6%)
  waiting for transfers between devices  0.79 us (1%)
    all_to_all x1, blocking collectives, on_device(): lax.all_to_all(spectra, ('tm', 'stn'), split_axis=0, concat_axis=0, tiled...  32.1 us
    pallas_call x2, Pallas kernels, band_spectra(): pl.pallas_call(kernel, out_shape=jax.ShapeDtypeStruct((2, rows, band), jn...  15.2 us
    dot_general x1, matrix products, on_device(): jnp.einsum('ki,kj->ij', both, stacked, preferred_element_type=jnp.float32)  4.67 us
    add x1, other arithmetic, band_tables(): pr[:, :, None, :] * b1[:, None, :, :]  4.58 us
    ppermute x1, starting transfers between devices, passed_along(): return lax.ppermute(x, axis, pairs)  4.09 us
    convert_element_type x1, other arithmetic, on_device(): spectra = jnp.stack([spec_re, spec_im], axis=2).astype(jnp.bfloat16)  2.21 us
    all_to_all x1, other arithmetic, on_device(): lax.all_to_all(spectra, ('tm', 'stn'), split_axis=0, concat_axis=0, tiled...  1.56 us
  transfers between devices with their start and end apart: 1, of which 1 were waited for; matrix products, arithmetic and copies ran while one was open for 0% of the time, Pallas kernels for 11%

profile of v3, /device:TPU:1, one launch (start us, length us, event | category | flops | bytes accessed | tf_op | source)
XLA Modules:
  0.0 71.9 jit_solution(13141740174523359862)
XLA Ops:
  0.0 0.0 copy-start.1
  0.0 0.0 copy-start
  0.0 1.0 %fusion.16 = (f32[2,128,256]{2,1,0:T(8,128)S(1)}, f32[2,128,256]{2,1,0:T(8,128)S(1)}) fusion(s32[2,256]{1,0:T(2,128)S(1)} %get-tuple-element.27), kind=kLoop, calls=%fused_computation.34 | loop fusion | flops 983040 | bytes 526336 | tf_op jit(solution)/shard_map/cos | solution.py:53
  1.1 0.3 negate_select_fusion.4
  1.4 4.6 %multiply_add_fusion = f32[2,128,32,256]{3,2,1,0:T(8,128)} fusion(f32[2,32,256]{2,1,0:T(8,128)S(1)} %get-tuple-element.24, f32[2,128,256]{2,1,0:T(8,128)S(1)} %get-tuple-element.26, f32[2,32,256]{2,1,0:T(8,128)S(1)} %get-tuple-element.23, f32[2,128,256]{2,1,0:T(8,128)S(1)} %get-tuple-element.25), kind=kLoop, calls=%fused_computation | loop fusion | flops 6291456 | bytes 9043968 | tf_op jit(solution)/shard_map/add | solution.py:57
  6.0 0.0 copy-done.1
  6.0 0.0 copy-done
  6.0 7.1 %shard_map.38 = f32[2,224,256]{2,1,0:T(8,128)S(1)} custom-call(bf16[32,65536]{1,0:T(8,128)(2,1)S(1)} %copy-done, f32[8,8192]{1,0:T(8,128)S(1)} %copy-done.1, f32[2,4096,256]{2,1,0:T(8,128)} %bitcast.55), custom_call_target="tpu_custom_call" | custom-call | tf_op jit(solution)/shard_map/pallas_call | solution.py:141
  13.1 0.0 copy-start.2
  13.1 4.1 %collective-permute-start = (f32[2,224,256]{2,1,0:T(8,128)S(1)}, f32[2,224,256]{2,1,0:T(8,128)S(1)}, u32[]{:S(2)}, u32[]{:S(2)}) collective-permute-start(f32[2,224,256]{2,1,0:T(8,128)S(1)} %shard_map.38), channel_id=1, source_target_pairs={{0,32},{32,64},{64,96},{96,128},{128,160},{160,192},{192,224},{1,3... | collective-permute-start | bytes 1376264 | tf_op jit(solution)/shard_map/ppermute | solution.py:20
  17.2 8.0 %shard_map.37 = f32[2,256,256]{2,1,0:T(8,128)S(1)} custom-call(bf16[32,65536]{1,0:T(8,128)(2,1)S(1)} %copy-done, f32[8,8192]{1,0:T(8,128)S(1)} %copy-done.1, f32[2,4096,256]{2,1,0:T(8,128)} %bitcast.56), custom_call_target="tpu_custom_call" | custom-call | tf_op jit(solution)/shard_map/pallas_call | solution.py:141
  25.3 0.0 copy-done.2
  25.3 0.1 copy.20
  25.4 0.1 copy.21
  25.5 0.1 copy.23
  25.6 0.8 %collective-permute-done = f32[2,224,256]{2,1,0:T(8,128)S(1)} collective-permute-done((f32[2,224,256]{2,1,0:T(8,128)S(1)}, f32[2,224,256]{2,1,0:T(8,128)S(1)}, u32[]{:S(2)}, u32[]{:S(2)}) %collective-permute-start) | collective-permute-done | bytes 458784 | tf_op jit(solution)/shard_map/ppermute | solution.py:20
  26.4 0.1 fusion.5
  26.5 0.1 fusion.10
  26.6 0.2 copy.24
  26.8 0.2 convert_element_type.39
  27.1 0.5 broadcast.255
  27.6 2.2 %reduce.3 = bf16[256,512]{1,0:T(8,128)(2,1)S(1)} reduce(bf16[256,1,512]{2,1,0:T(2,128)(2,1)S(1)} %convert_element_type.39, bf16[]{:T(256)} %broadcast.255), dimensions={1}, to_apply=%convert_element_type.39.reduce_sub_computation | reduce | bytes 524290 | tf_op jit(solution)/shard_map/convert_element_type | solution.py:187
  29.8 0.1 reshape.293
  29.9 32.1 %all_to_all.6 = bf16[256,2,256]{2,1,0:T(2,128)(2,1)S(1)} all-to-all(bf16[256,2,256]{2,1,0:T(2,128)(2,1)S(1)} %reshape.293), channel_id=1, replica_groups=mesh['tm'=8,'stn'=32] {'tm','stn'}, dimensions={0} | all-to-all | bytes 524288 | tf_op jit(solution)/shard_map/all_to_all | solution.py:189
  62.0 0.2 reshape.294
  62.2 1.6 %reduce.2 = bf16[256,512]{1,0:T(8,128)(2,1)S(1)} reduce(bf16[256,1,512]{2,1,0:T(2,128)(2,1)S(1)} %reshape.294, bf16[]{:T(256)} %constant.84), dimensions={1}, to_apply=%all_to_all.4.reduce_sub_computation | reduce | bytes 524290 | tf_op jit(solution)/shard_map/all_to_all | solution.py:189
  63.8 0.6 reshape.290
  64.4 0.1 fusion.28
  64.5 0.3 copy.26
  64.8 0.1 copy.28
  64.9 0.5 neg.28
  65.5 0.1 copy.27
  65.6 0.5 squeeze.14
  66.1 1.1 %reshape_reshape.3 = bf16[128,1024]{1,0:T(8,128)(2,1)S(1)} reshape(bf16[2,8,8,32,32]{4,3,2,1,0:T(8,128)(2,1)S(1)} %copy.26) | data formatting | bytes 524288 | tf_op jit(solution)/shard_map/reshape;reshape | solution.py:193
  67.2 4.7 %convolution_multiply_fusion = f32[2048,1024]{1,0:T(8,128)} fusion(bf16[128,1024]{1,0:T(8,128)(2,1)S(1)} %reshape_reshape.3, bf16[64,1024]{1,0:T(8,128)(2,1)S(1)} %neg.28, bf16[64,1024]{1,0:T(8,128)(2,1)S(1)} %squeeze.14), kind=kOutput, calls=%fused_computation.1 | convolution fusion | flops 540540928 | bytes 8912896 | tf_op jit(solution)/shard_map/ki,kj->ij/dot_general | solution.py:195
  (6 shorter events, 0.1 us)
Async XLA Ops:
  0.0 6.0 %copy-start.1 = (f32[8,8192]{1,0:T(8,128)S(1)}, f32[8,8192]{1,0:T(8,128)}, u32[]{:S(2)}) copy-start(f32[8,8192]{1,0:T(8,128)} %constant.83.clone.w_ref) | copy-start | bytes 786436
  0.0 6.0 %copy-start = (bf16[32,65536]{1,0:T(8,128)(2,1)S(1)}, bf16[32,65536]{1,0:T(8,128)(2,1)}, u32[]{:S(2)}) copy-start(bf16[32,65536]{1,0:T(8,128)(2,1)} %x_ref.3) | copy-start | bytes 12582916
  13.1 12.2 %copy-start.2 = (f32[2,32,256]{2,1,0:T(8,128)S(1)}, f32[2,32,256]{2,1,0:T(8,128)}, u32[]{:S(2)}) copy-start(f32[2,32,256]{2,1,0:T(8,128)} %param.6) | copy-start | bytes 196612
  13.1 13.3 %collective-permute-start = (f32[2,224,256]{2,1,0:T(8,128)S(1)}, f32[2,224,256]{2,1,0:T(8,128)S(1)}, u32[]{:S(2)}, u32[]{:S(2)}) collective-permute-start(f32[2,224,256]{2,1,0:T(8,128)S(1)} %shard_map.38), channel_id=1, source_target_pairs={{0,32},{32,64},{64,96},{96,128},{128,160},{160,192},{192,224},{1,3... | collective-permute-start | bytes 1376264 | tf_op jit(solution)/shard_map/ppermute | solution.py:20

commit v4 on v3

--- a/solution.py
+++ b/solution.py
@@ -106,7 +106,7 @@
     @pl.when(step == steps - 1)
     def _():
         copy_table.wait()
-        depth = 2048
+        depth = 4096
         f32 = jnp.float32
         out_ref[...] = jnp.zeros(out_ref.shape, f32)
 

time: 72 us -> 71.8 us (level)
  no operation moved by 1% of the time
where the time goes in v4:
time: 71.8 us; the launch traced here: 71.7 us
  blocking collectives  32.1 us (45%)
  Pallas kernels  14.8 us (21%)
  other arithmetic  10 us (14%)
  local copies, waits for them, and re-layouts  4.76 us (7%)
  matrix products  4.67 us (7%)
  starting transfers between devices  4.09 us (6%)
  waiting for transfers between devices  0.99 us (1%)
    all_to_all x1, blocking collectives, on_device(): lax.all_to_all(spectra, ('tm', 'stn'), split_axis=0, concat_axis=0, tiled...  32.1 us
    pallas_call x2, Pallas kernels, band_spectra(): pl.pallas_call(kernel, out_shape=jax.ShapeDtypeStruct((2, rows, band), jn...  14.8 us
    dot_general x1, matrix products, on_device(): jnp.einsum('ki,kj->ij', both, stacked, preferred_element_type=jnp.float32)  4.67 us
    add x1, other arithmetic, band_tables(): pr[:, :, None, :] * b1[:, None, :, :]  4.58 us
    ppermute x1, starting transfers between devices, passed_along(): return lax.ppermute(x, axis, pairs)  4.09 us
    convert_element_type x1, other arithmetic, on_device(): spectra = jnp.stack([spec_re, spec_im], axis=2).astype(jnp.bfloat16)  2.21 us
    all_to_all x1, other arithmetic, on_device(): lax.all_to_all(spectra, ('tm', 'stn'), split_axis=0, concat_axis=0, tiled...  1.56 us
  transfers between devices with their start and end apart: 1, of which 1 were waited for; matrix products, arithmetic and copies ran while one was open for 0% of the time, Pallas kernels for 11%

profile of v4, /device:TPU:1, one launch (start us, length us, event | category | flops | bytes accessed | tf_op | source)
XLA Modules:
  0.0 71.7 jit_solution(15903115318859121637)
XLA Ops:
  0.0 0.0 copy-start.1
  0.0 0.0 copy-start
  0.0 1.0 %fusion.16 = (f32[2,128,256]{2,1,0:T(8,128)S(1)}, f32[2,128,256]{2,1,0:T(8,128)S(1)}) fusion(s32[2,256]{1,0:T(2,128)S(1)} %get-tuple-element.27), kind=kLoop, calls=%fused_computation.34 | loop fusion | flops 983040 | bytes 526336 | tf_op jit(solution)/shard_map/cos | solution.py:53
  1.1 0.3 negate_select_fusion.4
  1.4 4.6 %multiply_add_fusion = f32[2,128,32,256]{3,2,1,0:T(8,128)} fusion(f32[2,32,256]{2,1,0:T(8,128)S(1)} %get-tuple-element.24, f32[2,128,256]{2,1,0:T(8,128)S(1)} %get-tuple-element.26, f32[2,32,256]{2,1,0:T(8,128)S(1)} %get-tuple-element.23, f32[2,128,256]{2,1,0:T(8,128)S(1)} %get-tuple-element.25), kind=kLoop, calls=%fused_computation | loop fusion | flops 6291456 | bytes 9043968 | tf_op jit(solution)/shard_map/add | solution.py:57
  6.0 0.0 copy-done.1
  6.0 0.0 copy-done
  6.0 6.9 %shard_map.38 = f32[2,224,256]{2,1,0:T(8,128)S(1)} custom-call(bf16[32,65536]{1,0:T(8,128)(2,1)S(1)} %copy-done, f32[8,8192]{1,0:T(8,128)S(1)} %copy-done.1, f32[2,4096,256]{2,1,0:T(8,128)} %bitcast.55), custom_call_target="tpu_custom_call" | custom-call | tf_op jit(solution)/shard_map/pallas_call | solution.py:141
  12.9 0.0 copy-start.2
  12.9 4.1 %collective-permute-start = (f32[2,224,256]{2,1,0:T(8,128)S(1)}, f32[2,224,256]{2,1,0:T(8,128)S(1)}, u32[]{:S(2)}, u32[]{:S(2)}) collective-permute-start(f32[2,224,256]{2,1,0:T(8,128)S(1)} %shard_map.38), channel_id=1, source_target_pairs={{0,32},{32,64},{64,96},{96,128},{128,160},{160,192},{192,224},{1,3... | collective-permute-start | bytes 1376264 | tf_op jit(solution)/shard_map/ppermute | solution.py:20
  17.0 7.8 %shard_map.37 = f32[2,256,256]{2,1,0:T(8,128)S(1)} custom-call(bf16[32,65536]{1,0:T(8,128)(2,1)S(1)} %copy-done, f32[8,8192]{1,0:T(8,128)S(1)} %copy-done.1, f32[2,4096,256]{2,1,0:T(8,128)} %bitcast.56), custom_call_target="tpu_custom_call" | custom-call | tf_op jit(solution)/shard_map/pallas_call | solution.py:141
  24.9 0.0 copy-done.2
  24.9 0.1 copy.20
  25.0 0.1 copy.21
  25.1 0.1 copy.23
  25.2 1.0 %collective-permute-done = f32[2,224,256]{2,1,0:T(8,128)S(1)} collective-permute-done((f32[2,224,256]{2,1,0:T(8,128)S(1)}, f32[2,224,256]{2,1,0:T(8,128)S(1)}, u32[]{:S(2)}, u32[]{:S(2)}) %collective-permute-start) | collective-permute-done | bytes 458784 | tf_op jit(solution)/shard_map/ppermute | solution.py:20
  26.2 0.1 fusion.5
  26.3 0.1 fusion.10
  26.4 0.2 copy.24
  26.6 0.2 convert_element_type.39
  26.9 0.5 broadcast.255
  27.4 2.2 %reduce.3 = bf16[256,512]{1,0:T(8,128)(2,1)S(1)} reduce(bf16[256,1,512]{2,1,0:T(2,128)(2,1)S(1)} %convert_element_type.39, bf16[]{:T(256)} %broadcast.255), dimensions={1}, to_apply=%convert_element_type.39.reduce_sub_computation | reduce | bytes 524290 | tf_op jit(solution)/shard_map/convert_element_type | solution.py:187
  29.6 0.1 reshape.293
  29.7 32.1 %all_to_all.6 = bf16[256,2,256]{2,1,0:T(2,128)(2,1)S(1)} all-to-all(bf16[256,2,256]{2,1,0:T(2,128)(2,1)S(1)} %reshape.293), channel_id=1, replica_groups=mesh['tm'=8,'stn'=32] {'tm','stn'}, dimensions={0} | all-to-all | bytes 524288 | tf_op jit(solution)/shard_map/all_to_all | solution.py:189
  61.8 0.2 reshape.294
  62.0 1.6 %reduce.2 = bf16[256,512]{1,0:T(8,128)(2,1)S(1)} reduce(bf16[256,1,512]{2,1,0:T(2,128)(2,1)S(1)} %reshape.294, bf16[]{:T(256)} %constant.84), dimensions={1}, to_apply=%all_to_all.4.reduce_sub_computation | reduce | bytes 524290 | tf_op jit(solution)/shard_map/all_to_all | solution.py:189
  63.6 0.6 reshape.290
  64.2 0.1 fusion.28
  64.3 0.3 copy.26
  64.6 0.1 copy.28
  64.7 0.5 neg.28
  65.3 0.1 copy.27
  65.4 0.5 squeeze.14
  65.9 1.1 %reshape_reshape.3 = bf16[128,1024]{1,0:T(8,128)(2,1)S(1)} reshape(bf16[2,8,8,32,32]{4,3,2,1,0:T(8,128)(2,1)S(1)} %copy.26) | data formatting | bytes 524288 | tf_op jit(solution)/shard_map/reshape;reshape | solution.py:193
  67.0 4.7 %convolution_multiply_fusion = f32[2048,1024]{1,0:T(8,128)} fusion(bf16[128,1024]{1,0:T(8,128)(2,1)S(1)} %reshape_reshape.3, bf16[64,1024]{1,0:T(8,128)(2,1)S(1)} %neg.28, bf16[64,1024]{1,0:T(8,128)(2,1)S(1)} %squeeze.14), kind=kOutput, calls=%fused_computation.1 | convolution fusion | flops 540540928 | bytes 8912896 | tf_op jit(solution)/shard_map/ki,kj->ij/dot_general | solution.py:195
  (6 shorter events, 0.1 us)
Async XLA Ops:
  0.0 6.0 %copy-start.1 = (f32[8,8192]{1,0:T(8,128)S(1)}, f32[8,8192]{1,0:T(8,128)}, u32[]{:S(2)}) copy-start(f32[8,8192]{1,0:T(8,128)} %constant.83.clone.w_ref) | copy-start | bytes 786436
  0.0 6.0 %copy-start = (bf16[32,65536]{1,0:T(8,128)(2,1)S(1)}, bf16[32,65536]{1,0:T(8,128)(2,1)}, u32[]{:S(2)}) copy-start(bf16[32,65536]{1,0:T(8,128)(2,1)} %x_ref.3) | copy-start | bytes 12582916
  12.9 12.0 %copy-start.2 = (f32[2,32,256]{2,1,0:T(8,128)S(1)}, f32[2,32,256]{2,1,0:T(8,128)}, u32[]{:S(2)}) copy-start(f32[2,32,256]{2,1,0:T(8,128)} %param.6) | copy-start | bytes 196612
  12.9 13.3 %collective-permute-start = (f32[2,224,256]{2,1,0:T(8,128)S(1)}, f32[2,224,256]{2,1,0:T(8,128)S(1)}, u32[]{:S(2)}, u32[]{:S(2)}) collective-permute-start(f32[2,224,256]{2,1,0:T(8,128)S(1)} %shard_map.38), channel_id=1, source_target_pairs={{0,32},{32,64},{64,96},{96,128},{128,160},{160,192},{192,224},{1,3... | collective-permute-start | bytes 1376264 | tf_op jit(solution)/shard_map/ppermute | solution.py:20
